TPU v7x, 512 devices: a whole 4x8x8 slice. The times are simulated.
512 devices in a mesh: own: 64 (over z, y), rep: 8 (over x, core).
Axes of the slice: x: 4, y: 8, z: 8, core: 2. Of those that a mesh axis runs over, the one named last changes fastest.
Arguments:
- tokens: bfloat16 [65536, 2560], P(('own', 'rep')), may hold values from -6 to 6
- cotangent: bfloat16 [65536, 2560], P(('own', 'rep')), may hold values from -6 to 6
- route: int32 [65536, 6], P(('own', 'rep')), may hold values from 0 to 159, all different within a row; in each aligned block of 128 rows (0 to 127, 128 to 255, ...) at most 6 rows name the same one
- gate_index: int32 [65536, 6], P(('own', 'rep')), may hold values from 0 to 255
- gate_table: float32 [256], replicated, may hold values from 0.1 to 1
- w_gate: bfloat16 [16384, 2560], P(('own', 'rep')), may hold values from -0.125 to 0.125
- w_up: bfloat16 [16384, 2560], P(('own', 'rep')), may hold values from -0.125 to 0.125
- w_down: bfloat16 [16384, 2560], P(('own', 'rep')), may hold values from -0.1875 to 0.1875
Outputs:
- grad_tokens: bfloat16 [65536, 2560], P(('own', 'rep'))
- grad_w_gate: float32 [16384, 2560], P(('own', 'rep'))
- grad_w_up: float32 [16384, 2560], P(('own', 'rep'))
- grad_w_down: float32 [16384, 2560], P(('own', 'rep'))
Inputs may be any that keep to these rules, and one draw needn't show every extreme that they name: `route`: each row names 6 different experts. Among the rows of one device no expert is named by more than 6 rows, and in some device some expert is named by exactly 6.
All inputs are finite; a program needn't handle non-finite values.
Results may differ from a plain program's by a relative error of at most 0.015.
Values may be sent and summed in bfloat16 or wider, within the bound.
No kernel may reach another device: no remote copies, remote signals or barrier semaphores. Data moves between devices by JAX's collectives and lax.ppermute only.
A program may use at most 64 MiB of HBM per device.

v0:
```python
import jax
import jax.numpy as jnp
from jax import lax
from jax.sharding import PartitionSpec as P

SPLIT = 4
CAP = 6


def silu_parts(pre_gate):
    sigmoid_value = jax.nn.sigmoid(pre_gate)
    return (pre_gate * sigmoid_value, sigmoid_value * (1.0 + pre_gate * (1.0 - sigmoid_value)))


def panel_terms(rows_x, rows_cot, panel_gate, panel_up, panel_down):
    pre_gate = jnp.dot(rows_x, panel_gate.T, preferred_element_type=jnp.float32)
    pre_up = jnp.dot(rows_x, panel_up.T, preferred_element_type=jnp.float32)
    active, slope_value = silu_parts(pre_gate)
    hidden = (active * pre_up).astype(jnp.bfloat16)
    hidden_delta = jnp.dot(rows_cot, panel_down.T, preferred_element_type=jnp.float32)
    gate_delta = (hidden_delta * pre_up * slope_value).astype(jnp.bfloat16)
    up_delta = (hidden_delta * active).astype(jnp.bfloat16)
    grad_rows = jnp.dot(gate_delta, panel_gate, preferred_element_type=jnp.float32) + jnp.dot(
        up_delta, panel_up, preferred_element_type=jnp.float32
    )
    grad_gate = jnp.dot(gate_delta.T, rows_x, preferred_element_type=jnp.float32)
    grad_up = jnp.dot(up_delta.T, rows_x, preferred_element_type=jnp.float32)
    grad_down = jnp.dot(hidden.T, rows_cot, preferred_element_type=jnp.float32)
    return (grad_rows, grad_gate, grad_up, grad_down)


def per_device(tokens, cotangent, route, gate_index, gate_table, w_gate, w_up, w_down):
    owners = lax.axis_size("own")
    experts_here = owners // SPLIT
    tok_count = tokens.shape[0]
    model_width = tokens.shape[1]
    choices_each = route.shape[1]
    table_hits = (
        gate_index[:, :, None] == jnp.arange(gate_table.shape[0], dtype=jnp.int32)[None, None, :]
    ).astype(jnp.float32)
    gate_values = jnp.sum(table_hits * gate_table[None, None, :], axis=2).reshape(-1)
    is_named = (
        route.reshape(-1)[:, None] == jnp.arange(experts_here, dtype=jnp.int32)[None, :]
    ).astype(jnp.int32)
    earlier = jnp.cumsum(is_named, axis=0) - is_named
    slot_hits = (
        is_named[:, :, None]
        * (earlier[:, :, None] == jnp.arange(CAP, dtype=jnp.int32)[None, None, :]).astype(jnp.int32)
    ).astype(jnp.float32)
    slot_hits = slot_hits.reshape(tok_count * choices_each, experts_here * CAP)
    select = slot_hits.reshape(tok_count, choices_each, experts_here * CAP).sum(axis=1)
    slot_gate = jnp.dot(
        gate_values, slot_hits, precision=lax.Precision.HIGHEST, preferred_element_type=jnp.float32
    )
    picker = select.astype(jnp.bfloat16)
    sent_x = jnp.dot(picker.T, tokens, preferred_element_type=jnp.float32).astype(jnp.bfloat16)
    sent_dy = jnp.dot(picker.T, cotangent, preferred_element_type=jnp.float32)
    sent_cot = (slot_gate[:, None] * sent_dy).astype(jnp.bfloat16)

    def fan_out(slot_rows):
        spread = jnp.broadcast_to(
            slot_rows.reshape(experts_here, 1, CAP, model_width),
            (experts_here, SPLIT, CAP, model_width),
        )
        return spread.reshape(owners, CAP, model_width)

    got_x, got_cot = (
        lax.all_to_all(fan_out(sent_x), "own", split_axis=0, concat_axis=0, tiled=True),
        lax.all_to_all(fan_out(sent_cot), "own", split_axis=0, concat_axis=0, tiled=True),
    )
    rows_x = got_x.reshape(owners * CAP, model_width)
    rows_cot = got_cot.reshape(owners * CAP, model_width)
    full_gate, full_up, full_down = (
        lax.all_gather(w_gate, "rep", axis=0, tiled=True),
        lax.all_gather(w_up, "rep", axis=0, tiled=True),
        lax.all_gather(w_down, "rep", axis=0, tiled=True),
    )
    grad_rows, grad_gate, grad_up, grad_down = panel_terms(
        rows_x, rows_cot, full_gate, full_up, full_down
    )
    block_rows = grad_rows.astype(jnp.bfloat16).reshape(owners, CAP, model_width)
    returned = lax.all_to_all(block_rows, "own", split_axis=0, concat_axis=0, tiled=True)
    per_slot = (
        returned.astype(jnp.float32)
        .reshape(experts_here, SPLIT, CAP, model_width)
        .sum(axis=1)
        .reshape(experts_here * CAP, model_width)
    )
    grad_tokens = jnp.dot(
        select, per_slot, precision=lax.Precision.HIGHEST, preferred_element_type=jnp.float32
    ).astype(jnp.bfloat16)
    stacked = jnp.stack([grad_gate, grad_up, grad_down]).astype(jnp.bfloat16).astype(jnp.float32)
    totals_all = lax.psum(stacked.astype(jnp.bfloat16), "rep").astype(jnp.float32)
    rows_each = stacked.shape[1] // lax.axis_size("rep")
    shares = lax.dynamic_slice_in_dim(totals_all, lax.axis_index("rep") * rows_each, rows_each, 1)
    return (grad_tokens, shares[0], shares[1], shares[2])


def solution(mesh):
    return jax.shard_map(
        per_device,
        mesh=mesh,
        in_specs=(
            P(("own", "rep"), None),
            P(("own", "rep"), None),
            P(("own", "rep"), None),
            P(("own", "rep"), None),
            P(),
            P(("own", "rep"), None),
            P(("own", "rep"), None),
            P(("own", "rep"), None),
        ),
        out_specs=(
            P(("own", "rep"), None),
            P(("own", "rep"), None),
            P(("own", "rep"), None),
            P(("own", "rep"), None),
        ),
        check_vma=False,
    )
```

profile of v0, /device:TPU:8, one launch (start us, length us, event | category | flops | bytes accessed | tf_op | source)
XLA Modules:
  0.0 346.3 jit_solution(16061698377593412336)
XLA Ops:
  7.2 0.9 copy.23
  8.0 0.1 eq.74
  8.2 0.1 eq.78
  8.3 1.7 reduce-window.6
  10.0 0.3 slice_reduce_fusion
  10.5 8.2 %eq.83 = s32[128,6,96]{1,0,2:T(8,128)} reshape(s32[768,16,6]{0,2,1:T(8,128)S(1)} %eq.82) | data formatting | bytes 589824 | tf_op jit(solution)/shard_map/eq | solution.py:48
  18.8 8.2 %mul.53 = s32[128,6,96]{1,0,2:T(8,128)} reshape(s32[768,16,6]{0,2,1:T(8,128)S(1)} %mul.52) | data formatting | bytes 589824 | tf_op jit(solution)/shard_map/mul | solution.py:47
  27.2 0.3 select_reduce_fusion
  27.5 0.1 copy.26
  27.6 0.1 reshape.136
  27.8 0.3 convolution_bitcast_fusion
  28.1 6.5 %convert_reduce_fusion = f32[128,96]{0,1:T(8,128)S(1)} fusion(s32[128,6,96]{1,0,2:T(8,128)} %mul.53, s32[128,6,96]{1,0,2:T(8,128)} %eq.83, s32[96]{0:T(128)S(1)} %eq.85), kind=kLoop, calls=%fused_computation | loop fusion | flops 282624 | bytes 639360 | tf_op jit(solution)/shard_map/reduce_sum | solution.py:51
  34.6 0.3 fusion.4
  34.8 0.2 broadcast_in_dim.8
  35.0 1.7 broadcast_in_dim.9
  36.7 16.6 %all-to-all-start = ((bf16[64,6,2560]{2,1,0:T(8,128)(2,1)}), bf16[64,6,2560]{2,1,0:T(8,128)(2,1)S(1)}, u32[]{:S(2)}, u32[]{:S(2)}) async-start(bf16[64,6,2560]{2,1,0:T(8,128)(2,1)} %bitcast.58), calls=%async_computation | async-start | bytes 5242880 | tf_op jit(solution)/shard_map/all_to_all | solution.py:69
  53.4 0.7 all-gather.6.cloned.1.call-update
  54.1 0.7 all-gather.8.cloned.1.call-update
  54.8 2.2 convolution_convert_fusion.4
  57.0 2.0 broadcast_in_dim.10
  59.0 59.7 %all-to-all-done = bf16[64,6,2560]{2,1,0:T(8,128)(2,1)S(1)} async-done(((bf16[64,6,2560]{2,1,0:T(8,128)(2,1)}), bf16[64,6,2560]{2,1,0:T(8,128)(2,1)S(1)}, u32[]{:S(2)}, u32[]{:S(2)}) %all-to-all-start) | async-done | bytes 1966112 | tf_op jit(solution)/shard_map/all_to_all | solution.py:69
  118.7 2.8 broadcast_in_dim.11
  121.5 19.6 %all-to-all-start.1 = ((bf16[64,6,2560]{2,1,0:T(8,128)(2,1)}), bf16[64,6,2560]{2,1,0:T(8,128)(2,1)}, u32[]{:S(2)}, u32[]{:S(2)}) async-start(bf16[64,6,2560]{2,1,0:T(8,128)(2,1)} %bitcast.59), calls=%async_computation.1 | async-start | bytes 5242880 | tf_op jit(solution)/shard_map/all_to_all | solution.py:68
  141.1 0.2 all-gather.4.cloned.1.call-start
  141.3 0.5 all-gather.4.cloned.1.call-update
  141.8 2.1 reshape.127
  143.9 60.3 %all-to-all-done.1 = bf16[64,6,2560]{2,1,0:T(8,128)(2,1)} async-done(((bf16[64,6,2560]{2,1,0:T(8,128)(2,1)}), bf16[64,6,2560]{2,1,0:T(8,128)(2,1)}, u32[]{:S(2)}, u32[]{:S(2)}) %all-to-all-start.1) | async-done | bytes 1966112 | tf_op jit(solution)/shard_map/all_to_all | solution.py:68
  204.3 2.8 reshape.129
  207.1 2.0 fusion.13
  209.1 2.8 fusion.14
  211.9 2.7 multiply_convert_fusion.1
  214.6 1.9 fusion.1
  216.5 0.7 fusion.15
  217.2 0.6 copy-done.3
  217.9 2.0 fusion
  219.9 4.1 %reshape.130 = bf16[64,6,2560]{2,1,0:T(8,128)(2,1)} reshape(bf16[384,2560]{1,0:T(8,128)(2,1)} %fusion) | data formatting | bytes 3932160 | tf_op jit(solution)/shard_map/reshape | solution.py:81
  224.0 19.7 %all-to-all-start.2 = ((bf16[64,6,2560]{2,1,0:T(8,128)(2,1)}), bf16[64,6,2560]{2,1,0:T(8,128)(2,1)}, u32[]{:S(2)}, u32[]{:S(2)}) async-start(bf16[64,6,2560]{2,1,0:T(8,128)(2,1)} %reshape.130), calls=%async_computation.2 | async-start | bytes 5242880 | tf_op jit(solution)/shard_map/all_to_all | solution.py:82
  243.8 0.9 fusion.2
  244.7 0.7 copy-done.1
  245.4 0.9 fusion.3
  246.3 0.4 copy-done.2
  246.7 2.1 pad_maximum_fusion
  248.8 84.3 %all-reduce.2.cloned.1.call-done = bf16[3,256,2560]{2,1,0:T(8,128)(2,1)} async-done(((bf16[3,256,2560]{2,1,0:T(8,128)(2,1)}), bf16[3,256,2560]{2,1,0:T(8,128)(2,1)}) %all-reduce.2.cloned.1.call-update) | async-done | bytes 3932176 | tf_op jit(solution)/shard_map/psum | solution.py:93
  333.1 1.1 dynamic-slice_convert_fusion
  334.2 1.0 slice_bitcast_fusion
  335.2 2.4 convert_reduce_fusion.1
  337.6 0.1 reshape.133
  337.7 2.1 convolution_convert_fusion.3
  (31 shorter events, 0.6 us)
Async XLA Ops:
  7.2 27.4 %copy-start = (bf16[128,2560]{1,0:T(8,128)(2,1)S(1)}, bf16[128,2560]{1,0:T(8,128)(2,1)}, u32[]{:S(2)}) copy-start(bf16[128,2560]{1,0:T(8,128)(2,1)} %param.9) | copy-start | bytes 1966084
  18.8 8.4 %copy-start.6 = (s32[128,6]{0,1:T(8,128)S(1)}, s32[128,6]{0,1:T(8,128)}, u32[]{:S(2)}) copy-start(s32[128,6]{0,1:T(8,128)} %param.11) | copy-start | bytes 9220
  18.8 8.4 %copy-start.7 = (f32[256]{0:T(256)S(1)}, f32[256]{0:T(256)}, u32[]{:S(2)}) copy-start(f32[256]{0:T(256)} %param.12) | copy-start | bytes 3076
  36.7 81.9 %all-to-all-start = ((bf16[64,6,2560]{2,1,0:T(8,128)(2,1)}), bf16[64,6,2560]{2,1,0:T(8,128)(2,1)S(1)}, u32[]{:S(2)}, u32[]{:S(2)}) async-start(bf16[64,6,2560]{2,1,0:T(8,128)(2,1)} %bitcast.58), calls=%async_computation | async-start | bytes 5242880 | tf_op jit(solution)/shard_map/all_to_all | solution.py:69
  53.3 153.7 %all-gather.6.cloned.1.call-start = ((), (), s32[]{:S(2)}) async-start(), calls=%async_computation.4 | async-start | bytes 1474560 | tf_op jit(solution)/shard_map/all_gather | solution.py:75
  54.1 155.0 %all-gather.8.cloned.1.call-start = ((), (), s32[]{:S(2)}) async-start(), calls=%async_computation.5 | async-start | bytes 1474560 | tf_op jit(solution)/shard_map/all_gather | solution.py:74
  121.5 82.8 %all-to-all-start.1 = ((bf16[64,6,2560]{2,1,0:T(8,128)(2,1)}), bf16[64,6,2560]{2,1,0:T(8,128)(2,1)}, u32[]{:S(2)}, u32[]{:S(2)}) async-start(bf16[64,6,2560]{2,1,0:T(8,128)(2,1)} %bitcast.59), calls=%async_computation.1 | async-start | bytes 5242880 | tf_op jit(solution)/shard_map/all_to_all | solution.py:68
  141.1 70.8 %all-gather.4.cloned.1.call-start = ((), (), s32[]{:S(2)}) async-start(), calls=%async_computation.3 | async-start | bytes 1474560 | tf_op jit(solution)/shard_map/all_gather | solution.py:76
  214.6 1.9 copy-start.4
  216.5 1.3 copy-start.3
  224.0 111.1 %all-to-all-start.2 = ((bf16[64,6,2560]{2,1,0:T(8,128)(2,1)}), bf16[64,6,2560]{2,1,0:T(8,128)(2,1)}, u32[]{:S(2)}, u32[]{:S(2)}) async-start(bf16[64,6,2560]{2,1,0:T(8,128)(2,1)} %reshape.130), calls=%async_computation.2 | async-start | bytes 5242880 | tf_op jit(solution)/shard_map/all_to_all | solution.py:82
  243.7 89.3 %all-reduce.2.cloned.1.call-start = ((), (), s32[]{:S(2)}) async-start(), calls=%async_computation.6 | async-start | bytes 7864320 | tf_op jit(solution)/shard_map/psum | solution.py:93
  243.8 1.5 copy-start.1
  243.8 1.6 copy-start.5
  245.4 1.3 copy-start.2
Sparse Core Ops, SparseCore 0:
  56.3 29.6 all-gather.5
  88.1 29.1 all-gather.7
  144.0 29.4 all-gather.3
  248.9 84.0 all-reduce.1
where the time goes:
time: 347 us; the launch traced here: 346 us
  waiting for transfers between devices  206 us (59%)
  starting transfers between devices  56.2 us (16%)
  local copies, waits for them, and re-layouts  36.9 us (11%)
  matrix products  18.7 us (5%)
  other arithmetic  14.3 us (4%)
  between operations  14 us (4%)
    psum x1, waiting for transfers between devices, per_device(): lax.psum(stacked.astype(jnp.bfloat16), 'rep').astype(jnp.float32)  84.3 us
    all_to_all x1, waiting for transfers between devices, per_device(): lax.all_to_all(fan_out(sent_x), 'own', split_axis=0, concat_axis=0, tiled...  60.3 us
    all_to_all x1, waiting for transfers between devices, per_device(): lax.all_to_all(fan_out(sent_cot), 'own', split_axis=0, concat_axis=0, til...  59.7 us
    all_to_all x1, starting transfers between devices, per_device(): lax.all_to_all(block_rows, 'own', split_axis=0, concat_axis=0, tiled=True)  19.7 us
    all_to_all x1, starting transfers between devices, per_device(): lax.all_to_all(fan_out(sent_x), 'own', split_axis=0, concat_axis=0, tiled...  19.6 us
    all_to_all x1, starting transfers between devices, per_device(): lax.all_to_all(fan_out(sent_cot), 'own', split_axis=0, concat_axis=0, til...  16.6 us
    eq x4, local copies, waits for them, and re-layouts, per_device(): earlier[:, :, None] == jnp.arange(CAP, dtype=jnp.int32)[None, None, :]  8.34 us
    mul x2, local copies, waits for them, and re-layouts, per_device(): is_named[:, :, None]  8.27 us
  transfers between devices with their start and end apart: 7, of which 3 were waited for; matrix products, arithmetic and copies ran while one was open for 7% of the time, Pallas kernels for 0%

commit v1 on v0

--- a/solution.py
+++ b/solution.py
@@ -90,7 +90,9 @@
         select, per_slot, precision=lax.Precision.HIGHEST, preferred_element_type=jnp.float32
     ).astype(jnp.bfloat16)
     stacked = jnp.stack([grad_gate, grad_up, grad_down]).astype(jnp.bfloat16).astype(jnp.float32)
-    totals_all = lax.psum(stacked.astype(jnp.bfloat16), "rep").astype(jnp.float32)
+    totals_all = jnp.sum(lax.all_gather(stacked.astype(jnp.bfloat16), "rep"), axis=0).astype(
+        jnp.float32
+    )
     rows_each = stacked.shape[1] // lax.axis_size("rep")
     shares = lax.dynamic_slice_in_dim(totals_all, lax.axis_index("rep") * rows_each, rows_each, 1)
     return (grad_tokens, shares[0], shares[1], shares[2])

time: 347 us -> 405 us (1.17)
  the two profiles are of different devices: /device:TPU:8 before, /device:TPU:1 now
where the time goes in v1:
time: 405 us; the launch traced here: 404 us
  waiting for transfers between devices  247 us (61%)
  starting transfers between devices  59.2 us (15%)
  local copies, waits for them, and re-layouts  38.5 us (10%)
  other arithmetic  27 us (7%)
  matrix products  17.8 us (4%)
  between operations  14 us (3%)
    all_gather x1, waiting for transfers between devices, per_device(): lax.all_gather(stacked.astype(jnp.bfloat16), 'rep')  70.2 us
    all_to_all x1, waiting for transfers between devices, per_device(): lax.all_to_all(block_rows, 'own', split_axis=0, concat_axis=0, tiled=True)  61.5 us
    all_to_all x1, waiting for transfers between devices, per_device(): lax.all_to_all(fan_out(sent_cot), 'own', split_axis=0, concat_axis=0, til...  58.3 us
    all_to_all x1, waiting for transfers between devices, per_device(): lax.all_to_all(fan_out(sent_x), 'own', split_axis=0, concat_axis=0, tiled...  55 us
    all_to_all x1, starting transfers between devices, per_device(): lax.all_to_all(fan_out(sent_cot), 'own', split_axis=0, concat_axis=0, til...  22.2 us
    all_to_all x1, starting transfers between devices, per_device(): lax.all_to_all(block_rows, 'own', split_axis=0, concat_axis=0, tiled=True)  19.4 us
    all_to_all x1, starting transfers between devices, per_device(): lax.all_to_all(fan_out(sent_x), 'own', split_axis=0, concat_axis=0, tiled...  17.3 us
    reduce_sum x1, other arithmetic, per_device(): jnp.sum(lax.all_gather(stacked.astype(jnp.bfloat16), 'rep'), axis=0)  13.6 us
  transfers between devices with their start and end apart: 7, of which 4 were waited for; matrix products, arithmetic and copies ran while one was open for 7% of the time, Pallas kernels for 0%

profile of v1, /device:TPU:1, one launch (start us, length us, event | category | flops | bytes accessed | tf_op | source)
XLA Modules:
  0.0 403.7 jit_solution(7479179454041629437)
XLA Ops:
  7.2 0.9 copy.23
  8.4 8.3 %mul.53 = s32[128,6,96]{1,0,2:T(8,128)} reshape(s32[768,16,6]{0,2,1:T(8,128)S(1)} %mul.52) | data formatting | bytes 589824 | tf_op jit(solution)/shard_map/mul | solution.py:47
  16.6 1.7 reduce-window.6
  18.3 0.3 slice_reduce_fusion
  18.8 8.2 %eq.83 = s32[128,6,96]{1,0,2:T(8,128)} reshape(s32[768,16,6]{0,2,1:T(8,128)S(1)} %eq.82) | data formatting | bytes 589824 | tf_op jit(solution)/shard_map/eq | solution.py:48
  27.1 6.4 %convert_reduce_fusion = f32[128,96]{0,1:T(8,128)S(1)} fusion(s32[128,6,96]{1,0,2:T(8,128)} %mul.53, s32[128,6,96]{1,0,2:T(8,128)} %eq.83, s32[96]{0:T(128)S(1)} %eq.85), kind=kLoop, calls=%fused_computation | loop fusion | flops 282624 | bytes 639360 | tf_op jit(solution)/shard_map/reduce_sum | solution.py:51
  33.5 0.3 convolution_convert_fusion.4
  33.8 0.2 broadcast_in_dim.10
  34.0 1.7 broadcast_in_dim.11
  35.7 17.3 %all-to-all-start.1 = ((bf16[64,6,2560]{2,1,0:T(8,128)(2,1)}), bf16[64,6,2560]{2,1,0:T(8,128)(2,1)S(1)}, u32[]{:S(2)}, u32[]{:S(2)}) async-start(bf16[64,6,2560]{2,1,0:T(8,128)(2,1)} %bitcast.58), calls=%async_computation.1 | async-start | bytes 5242880 | tf_op jit(solution)/shard_map/all_to_all | solution.py:68
  53.0 0.7 all-gather.9.cloned.1.call-update
  53.7 0.3 select_reduce_fusion
  54.3 0.8 convert_element_type.73
  55.1 1.3 convolution_bitcast_fusion
  56.4 2.2 fusion.4
  58.6 1.2 broadcast_in_dim.8
  59.8 55.0 %all-to-all-done.1 = bf16[64,6,2560]{2,1,0:T(8,128)(2,1)S(1)} async-done(((bf16[64,6,2560]{2,1,0:T(8,128)(2,1)}), bf16[64,6,2560]{2,1,0:T(8,128)(2,1)S(1)}, u32[]{:S(2)}, u32[]{:S(2)}) %all-to-all-start.1) | async-done | bytes 1966112 | tf_op jit(solution)/shard_map/all_to_all | solution.py:68
  114.8 1.8 broadcast_in_dim.9
  116.6 0.4 copy-done.2
  117.1 22.2 %all-to-all-start = ((bf16[64,6,2560]{2,1,0:T(8,128)(2,1)}), bf16[64,6,2560]{2,1,0:T(8,128)(2,1)}, u32[]{:S(2)}, u32[]{:S(2)}) async-start(bf16[64,6,2560]{2,1,0:T(8,128)(2,1)} %bitcast.59), calls=%async_computation | async-start | bytes 5242880 | tf_op jit(solution)/shard_map/all_to_all | solution.py:69
  139.3 0.7 all-gather.7.cloned.1.call-update
  140.1 0.7 all-gather.5.cloned.1.call-update
  140.8 0.2 all-gather.11.cloned.1.call-start
  141.0 2.8 reshape.177
  143.8 58.3 %all-to-all-done = bf16[64,6,2560]{2,1,0:T(8,128)(2,1)} async-done(((bf16[64,6,2560]{2,1,0:T(8,128)(2,1)}), bf16[64,6,2560]{2,1,0:T(8,128)(2,1)}, u32[]{:S(2)}, u32[]{:S(2)}) %all-to-all-start) | async-done | bytes 1966112 | tf_op jit(solution)/shard_map/all_to_all | solution.py:69
  202.1 4.1 %reshape.175 = bf16[384,2560]{1,0:T(8,128)(2,1)} reshape(bf16[64,6,2560]{2,1,0:T(8,128)(2,1)} %all-to-all-done) | data formatting | bytes 3932160 | tf_op jit(solution)/shard_map/reshape | solution.py:72
  206.2 2.0 fusion.14
  208.3 2.2 fusion.13
  210.5 2.0 fusion.3
  212.5 2.7 multiply_convert_fusion.1
  215.2 0.9 fusion.2
  216.1 0.9 fusion.1
  217.0 0.4 copy-done.4
  217.4 2.1 pad_maximum_fusion
  219.5 1.3 copy-done.6
  220.8 0.7 fusion.15
  221.5 0.6 copy-done.5
  222.1 0.7 fusion
  222.8 2.3 reshape.178
  225.2 19.4 %all-to-all-start.2 = ((bf16[64,6,2560]{2,1,0:T(8,128)(2,1)}), bf16[64,6,2560]{2,1,0:T(8,128)(2,1)S(1)}, u32[]{:S(2)}, u32[]{:S(2)}) async-start(bf16[64,6,2560]{2,1,0:T(8,128)(2,1)} %reshape.178), calls=%async_computation.2 | async-start | bytes 5242880 | tf_op jit(solution)/shard_map/all_to_all | solution.py:82
  244.6 61.5 %all-to-all-done.2 = bf16[64,6,2560]{2,1,0:T(8,128)(2,1)S(1)} async-done(((bf16[64,6,2560]{2,1,0:T(8,128)(2,1)}), bf16[64,6,2560]{2,1,0:T(8,128)(2,1)S(1)}, u32[]{:S(2)}, u32[]{:S(2)}) %all-to-all-start.2) | async-done | bytes 1966112 | tf_op jit(solution)/shard_map/all_to_all | solution.py:82
  306.1 1.6 convert_reduce_fusion.1
  307.7 1.5 reshape.181
  309.2 2.1 convolution_convert_fusion.3
  311.3 70.2 %all-gather.11.cloned.1.call-done = bf16[8,3,256,2560]{3,2,1,0:T(8,128)(2,1)} async-done(((bf16[1,3,256,2560]{3,2,1,0:T(8,128)(2,1)}), bf16[8,3,256,2560]{3,2,1,0:T(8,128)(2,1)}) %all-gather.11.cloned.1.call-update) | async-done | bytes 31457296 | tf_op jit(solution)/shard_map/all_gather | solution.py:93
  381.5 13.6 %reduce_sum.42 = bf16[3,256,2560]{2,1,0:T(8,128)(2,1)} reduce(bf16[8,3,256,2560]{3,2,1,0:T(8,128)(2,1)} %all-gather.11.cloned.1.call-done, bf16[]{:T(256)} %constant.17.clone.1), dimensions={0}, to_apply=%region_5.6 | reduce | flops 13762560 | bytes 35389440 | tf_op jit(solution)/shard_map/reduce_sum | solution.py:93
  395.1 1.1 dynamic-slice_convert_fusion
  396.2 1.0 slice_bitcast_fusion
  (36 shorter events, 1.0 us)
Async XLA Ops:
  7.2 26.3 %copy-start = (bf16[128,2560]{1,0:T(8,128)(2,1)S(1)}, bf16[128,2560]{1,0:T(8,128)(2,1)}, u32[]{:S(2)}) copy-start(bf16[128,2560]{1,0:T(8,128)(2,1)} %param.8) | copy-start | bytes 1966084
  35.7 18.0 %copy-start.8 = (s32[128,6]{0,1:T(8,128)S(1)}, s32[128,6]{0,1:T(8,128)}, u32[]{:S(2)}) copy-start(s32[128,6]{0,1:T(8,128)} %param.11) | copy-start | bytes 9220
  35.7 18.0 %copy-start.9 = (f32[256]{0:T(256)S(1)}, f32[256]{0:T(256)}, u32[]{:S(2)}) copy-start(f32[256]{0:T(256)} %param.12) | copy-start | bytes 3076
  35.7 79.1 %all-to-all-start.1 = ((bf16[64,6,2560]{2,1,0:T(8,128)(2,1)}), bf16[64,6,2560]{2,1,0:T(8,128)(2,1)S(1)}, u32[]{:S(2)}, u32[]{:S(2)}) async-start(bf16[64,6,2560]{2,1,0:T(8,128)(2,1)} %bitcast.58), calls=%async_computation.1 | async-start | bytes 5242880 | tf_op jit(solution)/shard_map/all_to_all | solution.py:68
  52.9 153.3 %all-gather.9.cloned.1.call-start = ((), (), s32[]{:S(2)}) async-start(), calls=%async_computation.5 | async-start | bytes 1474560 | tf_op jit(solution)/shard_map/all_gather | solution.py:74
  114.8 2.3 copy-start.2
  117.1 85.0 %all-to-all-start = ((bf16[64,6,2560]{2,1,0:T(8,128)(2,1)}), bf16[64,6,2560]{2,1,0:T(8,128)(2,1)}, u32[]{:S(2)}, u32[]{:S(2)}) async-start(bf16[64,6,2560]{2,1,0:T(8,128)(2,1)} %bitcast.59), calls=%async_computation | async-start | bytes 5242880 | tf_op jit(solution)/shard_map/all_to_all | solution.py:69
  139.3 69.0 %all-gather.7.cloned.1.call-start = ((), (), s32[]{:S(2)}) async-start(), calls=%async_computation.4 | async-start | bytes 1474560 | tf_op jit(solution)/shard_map/all_gather | solution.py:75
  140.0 72.5 %all-gather.5.cloned.1.call-start = ((), (), s32[]{:S(2)}) async-start(), calls=%async_computation.3 | async-start | bytes 1474560 | tf_op jit(solution)/shard_map/all_gather | solution.py:76
  140.8 240.7 %all-gather.11.cloned.1.call-start = ((), (), s32[]{:S(2)}) async-start(), calls=%async_computation.6 | async-start | bytes 35389440 | tf_op jit(solution)/shard_map/all_gather | solution.py:93
  208.3 2.2 copy-start.3
  210.5 2.0 copy-start.7
  216.1 1.3 copy-start.4
  219.5 1.3 copy-start.6
  220.8 1.3 copy-start.5
  225.2 80.9 %all-to-all-start.2 = ((bf16[64,6,2560]{2,1,0:T(8,128)(2,1)}), bf16[64,6,2560]{2,1,0:T(8,128)(2,1)S(1)}, u32[]{:S(2)}, u32[]{:S(2)}) async-start(bf16[64,6,2560]{2,1,0:T(8,128)(2,1)} %reshape.178), calls=%async_computation.2 | async-start | bytes 5242880 | tf_op jit(solution)/shard_map/all_to_all | solution.py:82
  381.5 15.7 %copy-start.1 = (bf16[128,2560]{1,0:T(8,128)(2,1)S(1)}, bf16[128,2560]{1,0:T(8,128)(2,1)}, u32[]{:S(2)}) copy-start(bf16[128,2560]{1,0:T(8,128)(2,1)} %param.8) | copy-start | bytes 1966084
Sparse Core Ops, SparseCore 0:
  55.9 30.4 all-gather.8
  142.2 31.2 all-gather.6
  175.6 29.0 all-gather.4
  219.6 161.7 all-gather.10
